TPU v7x, 256 devices: a whole 4x4x8 slice. The times are simulated.
256 devices in a mesh: attn: 32 (over z, y), expert: 4 (over x), rep: 2 (over core).
Axes of the slice: x: 4, y: 4, z: 8, core: 2. Of those that a mesh axis runs over, the one named last changes fastest.
Arguments:
- queries: bfloat16 [256, 73728], P('attn', ('expert', 'rep')), may hold values from -120 to 120
- new_latent: bfloat16 [256, 576], P('attn'), may hold values from -6 to 6
- cache_pool: bfloat16 [16384, 576], P('attn'), may hold values from -6 to 6
- local_len: int32 [32, 4], P('attn'), may hold values from 1 to 384, 512 in all within a row
- spill_cache: bfloat16 [1024, 16, 576], P('attn'), may hold values from -6 to 6
- spill_owner: int32 [1024], replicated, may hold values from -1 to 127, as said below
- w_uv: bfloat16 [128, 512, 128], P(('expert', 'rep')), may hold values from -0.25 to 0.25
- w_o: bfloat16 [16384, 7168], P(('expert', 'rep'), 'attn'), may hold values from -0.046875 to 0.046875
- residual: bfloat16 [256, 7168], P(None, 'attn'), may hold values from -3 to 3
- norm_gain: float32 [7168], replicated, may hold values from 0.5 to 1.5
- route_ids: int32 [256, 4], replicated, may hold values from 0 to 15, all different within a row; in each aligned block of 128 rows (0 to 127, 128 to 255, ...) at most 40 rows name the same one
- route_scores: float32 [256, 4], replicated, may hold values from 0.05 to 1
- w_gate: bfloat16 [7168, 32768], P(None, ('attn', 'expert')), may hold values from -0.0625 to 0.0625
- w_up: bfloat16 [7168, 32768], P(None, ('attn', 'expert')), may hold values from -0.0625 to 0.0625
- w_down: bfloat16 [32768, 7168], P(('attn', 'expert')), may hold values from -0.125 to 0.125
Outputs:
- mixed: bfloat16 [256, 7168], P('rep', ('attn', 'expert'))
Inputs may be any that keep to these rules, and one draw needn't show every extreme that they name: Each row of local_len sums to 512. `spill_owner`: each entry is -1 or the number of a request that lives on another index of attn than the block's slot. The slots of one index of attn hold at most 2 blocks of the requests of any one other index, and some index holds exactly 2 for some other index in every draw. `route_ids`: the token rows fall into 2 aligned blocks of 128 rows in order (2 being the size of rep); in each block no expert is named by more than 40 rows, and in some block one is named by exactly 40.
All inputs are finite; a program needn't handle non-finite values.
Results may differ from a plain program's by a relative error of at most 0.025.
Values may be sent and summed in bfloat16 or wider, within the bound.
No kernel may reach another device: no remote copies, remote signals or barrier semaphores. Data moves between devices by JAX's collectives and lax.ppermute only.
A program may use at most 128 MiB of HBM per device.

v0:
```python
import jax
import jax.numpy as jnp
from jax import lax
from jax.sharding import PartitionSpec as P

ROPE = 64
VH = 128
EXPERTS = 16
TOP = 4
MAXLOC = 384
CAP = 2
floor_score = -1e30
scale_out = 2.5


def expert_tables(route_ids, part_index, part_count, capacity):
    row_count = route_ids.shape[0] // part_count
    route_part = lax.dynamic_slice_in_dim(route_ids, part_index * row_count, row_count, 0)
    member = jnp.any(
        route_part[:, :, None] == jnp.arange(EXPERTS, dtype=jnp.int32)[None, None, :], axis=1
    )
    order_rank = jnp.cumsum(member.astype(jnp.int32), axis=0) - 1
    slot_ids = jnp.arange(capacity, dtype=jnp.int32)
    slot_hit = member[None, :, :] & (order_rank[None, :, :] == slot_ids[:, None, None])
    place_ids = jnp.arange(row_count, dtype=jnp.int32)
    slot_token = jnp.sum(jnp.where(slot_hit, place_ids[None, :, None], 0), axis=1)
    filled = jnp.any(slot_hit, axis=1)
    return (slot_token.T, filled.T, route_part)


def per_device(
    queries,
    new_latent,
    cache_pool,
    local_len,
    spill_cache,
    spill_owner,
    w_uv,
    w_o,
    residual,
    norm_gain,
    route_ids,
    route_scores,
    w_gate,
    w_up,
    w_down,
):
    n_attn = lax.axis_size("attn")
    n_expert = lax.axis_size("expert")
    n_rep = lax.axis_size("rep")
    attn_here = lax.axis_index("attn")
    expert_here = lax.axis_index("expert")
    rep_here = lax.axis_index("rep")
    req_count = local_len.shape[1]
    head_count = w_uv.shape[0]
    row_width = new_latent.shape[1]
    lat_width = w_uv.shape[1]
    score_scale = float(VH + ROPE) ** (-0.5)
    query_rows = queries.reshape(req_count, 2, head_count, row_width)
    lengths = local_len[0]
    starts = jnp.cumsum(lengths) - lengths
    padded = jnp.concatenate([cache_pool, jnp.zeros((MAXLOC, row_width), cache_pool.dtype)], axis=0)
    windows = jax.vmap(lambda start_one: lax.dynamic_slice_in_dim(padded, start_one, MAXLOC, 0))(
        starts
    )
    local_scores = (
        jnp.einsum("rthc,rkc->rthk", query_rows, windows, preferred_element_type=jnp.float32)
        * score_scale
    )
    inside = jnp.arange(MAXLOC)[None, :] < lengths[:, None]
    local_scores = jnp.where(inside[:, None, None, :], local_scores, floor_score)
    fresh_keys = new_latent.reshape(req_count, 2, row_width)
    fresh_scores = (
        jnp.einsum("rthc,rkc->rthk", query_rows, fresh_keys, preferred_element_type=jnp.float32)
        * score_scale
    )
    causal = jnp.arange(2)[None, :] <= jnp.arange(2)[:, None]
    fresh_scores = jnp.where(causal[None, :, None, :], fresh_scores, floor_score)
    spill_count = spill_cache.shape[0]
    directory = spill_owner.reshape(n_attn, spill_count)
    owner_dev = jnp.where(directory >= 0, directory // req_count, -1)
    earlier = jnp.arange(spill_count)[:, None] > jnp.arange(spill_count)[None, :]
    same_owner = owner_dev[:, :, None] == owner_dev[:, None, :]
    order_rank = jnp.sum(same_owner & earlier[None, :, :], axis=2)
    slot_ids = jnp.arange(CAP)
    own_row = owner_dev[attn_here]
    own_rank = order_rank[attn_here]
    pick_slot = (own_row[None, None, :] == jnp.arange(n_attn)[:, None, None]) & (
        own_rank[None, None, :] == slot_ids[None, :, None]
    )
    outgoing = jnp.einsum(
        "dks,sbc->dkbc",
        pick_slot.astype(jnp.bfloat16),
        spill_cache,
        preferred_element_type=jnp.float32,
    ).astype(jnp.bfloat16)
    incoming = lax.all_to_all(outgoing, "attn", split_axis=0, concat_axis=0, tiled=True)
    mine_slot = (owner_dev[:, None, :] == attn_here) & (
        order_rank[:, None, :] == slot_ids[None, :, None]
    )
    present = jnp.any(mine_slot, axis=2).reshape(-1)
    request = jnp.sum(
        jnp.where(mine_slot, directory[:, None, :] - attn_here * req_count, 0), axis=2
    ).reshape(-1)
    blocks = incoming.reshape(n_attn * CAP, incoming.shape[2], row_width)
    slot_query = jnp.take(query_rows, request, axis=0)
    spill_scores = (
        jnp.einsum("nthc,nbc->nthb", slot_query, blocks, preferred_element_type=jnp.float32)
        * score_scale
    )
    spill_scores = jnp.where(present[:, None, None, None], spill_scores, floor_score)
    belong = (request[None, :] == jnp.arange(req_count)[:, None]) & present[None, :]
    spill_top = jnp.max(
        jnp.where(belong[:, :, None, None], jnp.max(spill_scores, axis=3)[None], floor_score),
        axis=1,
    )
    row_top = jnp.maximum(
        jnp.maximum(jnp.max(local_scores, axis=3), jnp.max(fresh_scores, axis=3)), spill_top
    )
    local_weight = jnp.exp(local_scores - row_top[..., None])
    fresh_weight = jnp.exp(fresh_scores - row_top[..., None])
    spill_weight = jnp.exp(spill_scores - jnp.take(row_top, request, axis=0)[..., None])
    spill_weight = jnp.where(present[:, None, None, None], spill_weight, 0.0)
    belong_f = belong.astype(jnp.float32)
    denominator = jnp.sum(local_weight, axis=3) + jnp.sum(fresh_weight, axis=3)
    denominator = denominator + jnp.einsum(
        "rn,nth->rth", belong_f, jnp.sum(spill_weight, axis=3), precision=lax.Precision.HIGHEST
    )
    numerator = jnp.einsum(
        "rthk,rkc->rthc",
        local_weight.astype(jnp.bfloat16),
        windows[:, :, :lat_width],
        preferred_element_type=jnp.float32,
    )
    numerator = numerator + jnp.einsum(
        "rthk,rkc->rthc",
        fresh_weight.astype(jnp.bfloat16),
        fresh_keys[:, :, :lat_width],
        preferred_element_type=jnp.float32,
    )
    spill_numer = jnp.einsum(
        "nthb,nbc->nthc",
        spill_weight.astype(jnp.bfloat16),
        blocks[:, :, :lat_width],
        preferred_element_type=jnp.float32,
    )
    numerator = numerator + jnp.einsum(
        "rn,nthc->rthc", belong_f, spill_numer, precision=lax.Precision.HIGHEST
    )
    attended = (numerator / denominator[..., None]).astype(jnp.bfloat16)
    values = jnp.einsum(
        "rthc,hcv->rthv", attended, w_uv, preferred_element_type=jnp.float32
    ).astype(jnp.bfloat16)
    values = values.reshape(2 * req_count, head_count * w_uv.shape[2])
    partial_cols = jnp.dot(
        lax.all_gather(values, "attn", axis=0, tiled=True), w_o, preferred_element_type=jnp.float32
    )
    attn_cols = lax.psum(partial_cols.astype(jnp.bfloat16), ("expert", "rep")).astype(jnp.float32)
    hidden_cols = (residual.astype(jnp.float32) + attn_cols).astype(jnp.bfloat16)
    rows_part = route_ids.shape[0] // n_rep
    capacity = rows_part * TOP // EXPERTS * 5 // 4
    shards = n_attn * n_expert // EXPERTS
    slot_token, filled, route_part = expert_tables(route_ids, rep_here, n_rep, capacity)
    part_cols = lax.dynamic_slice_in_dim(hidden_cols, rep_here * rows_part, rows_part, 0)
    dest_expert = (jnp.arange(n_attn) * n_expert + expert_here) // shards
    send_rows = jnp.take(slot_token, dest_expert, axis=0)
    send_ok = jnp.take(filled, dest_expert, axis=0)
    outgoing_rows = jnp.where(
        send_ok[:, :, None], jnp.take(part_cols, send_rows, axis=0), jnp.zeros((), jnp.bfloat16)
    )
    outgoing_rows = outgoing_rows[:, :, None, :]
    received = lax.all_to_all(outgoing_rows, "attn", split_axis=0, concat_axis=2, tiled=True)
    item_count = received.shape[1]
    full_rows = received.reshape(item_count, -1)
    widened = full_rows.astype(jnp.float32)
    normed = (
        widened * lax.rsqrt(jnp.mean(widened * widened, axis=1, keepdims=True) + 1e-06) * norm_gain
    ).astype(jnp.bfloat16)
    gate_proj = jnp.dot(normed, w_gate, preferred_element_type=jnp.float32)
    up_proj = jnp.dot(normed, w_up, preferred_element_type=jnp.float32)
    activated = (jax.nn.silu(gate_proj) * up_proj).astype(jnp.bfloat16)
    result = jnp.dot(activated, w_down, preferred_element_type=jnp.float32)
    returned_block = lax.all_to_all(
        result.reshape(1, item_count, n_attn * n_expert, -1).astype(jnp.bfloat16),
        ("attn", "expert"),
        split_axis=2,
        concat_axis=0,
        tiled=True,
    ).astype(jnp.float32)
    returned = returned_block.reshape(n_attn * n_expert, item_count, -1)
    share_part = lax.dynamic_slice_in_dim(route_scores, rep_here * rows_part, rows_part, 0)
    share_part = share_part / jnp.sum(share_part, axis=1, keepdims=True)
    share_table = jnp.sum(
        jnp.where(
            route_part[:, :, None] == jnp.arange(EXPERTS, dtype=jnp.int32)[None, None, :],
            share_part[:, :, None],
            0.0,
        ),
        axis=1,
    )
    source_expert = jnp.arange(n_attn * n_expert) // shards
    back_rows = jnp.take(slot_token, source_expert, axis=0)
    back_ok = jnp.take(filled, source_expert, axis=0)
    weight_coef = (
        jnp.where(back_ok, share_table[back_rows, source_expert[:, None]], 0.0) * scale_out
    )
    sub_cols = returned.shape[2]
    weighted = (weight_coef[:, :, None] * returned).reshape(-1, sub_cols)
    routed = jax.ops.segment_sum(weighted, back_rows.reshape(-1), num_segments=rows_part)
    own_cols = lax.dynamic_slice_in_dim(part_cols, expert_here * sub_cols, sub_cols, 1)
    return (own_cols.astype(jnp.float32) + routed).astype(jnp.bfloat16)


def solution(mesh):
    return jax.shard_map(
        per_device,
        mesh=mesh,
        in_specs=(
            P("attn", ("expert", "rep")),
            P("attn", None),
            P("attn", None),
            P("attn", None),
            P("attn", None, None),
            P(),
            P(("expert", "rep"), None, None),
            P(("expert", "rep"), "attn"),
            P(None, "attn"),
            P(),
            P(),
            P(),
            P(None, ("attn", "expert")),
            P(None, ("attn", "expert")),
            P(("attn", "expert"), None),
        ),
        out_specs=P("rep", ("attn", "expert")),
        check_vma=False,
    )
```

profile of v0, /device:TPU:1, one launch (start us, length us, event | category | flops | bytes accessed | tf_op | source)
XLA Modules:
  0.0 364.1 jit_solution(18145144369421537697)
XLA Ops:
  6.5 0.9 reshape.649
  7.5 0.8 convert_reduce_fusion
  8.3 1.6 convolution_convert_fusion.1
  9.9 1.5 copy.175
  11.4 12.3 %all-to-all-start = ((bf16[32,2,16,576]{3,2,1,0:T(8,128)(2,1)}), bf16[32,2,16,576]{3,2,1,0:T(8,128)(2,1)}, u32[]{:S(2)}, u32[]{:S(2)}) async-start(bf16[32,2,16,576]{3,2,1,0:T(8,128)(2,1)} %copy.175), calls=%async_computation | async-start | bytes 2621440 | tf_op jit(solution)/shard_map/all_to_all | solution.py:97
  25.2 1.1 copy.169
  26.3 2.4 gather_fusion
  28.6 1.2 concatenate.9
  30.3 8.1 %while.1 = (s32[]{:T(128)}, bf16[896,576]{1,0:T(8,128)(2,1)S(1)}, s32[4,2]{0,1:T(2,128)S(1)}, bf16[4,384,576]{2,1,0:T(8,128)(2,1)}, s32[]{:T(128)}) while((s32[]{:T(128)}, bf16[896,576]{1,0:T(8,128)(2,1)S(1)}, s32[4,2]{0,1:T(2,128)S(1)}, bf16[4,384,576]{2,1,0:T(8,128)(2,1)}, s32[]{:T(128)}) %tuple.22), condition=%wide.while_cond, body=%wide.while_body.sunk | while | flops 2 | bytes 935001 | solution.py:63
  30.9 1.5 bitcast_dynamic-update-slice_fusion.2
  32.9 1.5 bitcast_dynamic-update-slice_fusion.2
  34.9 1.4 bitcast_dynamic-update-slice_fusion.2
  36.9 1.5 bitcast_dynamic-update-slice_fusion.2
  38.4 3.0 fusion.93
  41.3 14.2 %all-to-all-done = bf16[32,2,16,576]{3,2,1,0:T(8,128)(2,1)} async-done(((bf16[32,2,16,576]{3,2,1,0:T(8,128)(2,1)}), bf16[32,2,16,576]{3,2,1,0:T(8,128)(2,1)}, u32[]{:S(2)}, u32[]{:S(2)}) %all-to-all-start) | async-done | bytes 1179680 | tf_op jit(solution)/shard_map/all_to_all | solution.py:97
  55.6 6.0 %fusion.2 = f32[64,2,16,16]{2,3,1,0:T(8,128)S(1)} fusion(bf16[64,16,576,1]{2,1,3,0:T(8,128)(2,1)} %bitcast.13, bf16[64,2,16,576]{3,2,1,0:T(8,128)(2,1)} %gather_fusion, pred[64]{0:T(512)(128)(4,1)S(1)} %compare_and_fusion.3), kind=kOutput, calls=%fused_computation.14 | convolution fusion | flops 38928384 | bytes 3670080 | tf_op jit(solution)/shard_map/nthc,nbc->nthb/dot_general | solution.py:108
  63.1 1.1 fusion.51
  64.7 0.9 copy.180
  65.5 1.9 fusion.43
  67.5 3.8 %fusion = f32[4,2,16,512]{3,0,2,1:T(4,128)S(1)} fusion(f32[64,2,16,512]{3,2,1,0:T(8,128)S(1)} %fusion.43, pred[4,64]{1,0:T(4,128)(4,1)S(1)} %fusion.81), kind=kOutput, calls=%fused_computation.12 | convolution fusion | flops 50331648 | bytes 4456704 | tf_op jit(solution)/shard_map/rn,nthc->rthc/dot_general | solution.py:147
  73.7 0.8 select_reduce_fusion
  75.4 0.8 fusion.47
  76.9 67.3 %all-gather.2.cloned.1.call-done = bf16[256,2048]{1,0:T(8,128)(2,1)} async-done(((bf16[8,2048]{1,0:T(8,128)(2,1)}), bf16[256,2048]{1,0:T(8,128)(2,1)}) %all-gather.2.cloned.1.call-update) | async-done | bytes 1048592 | tf_op jit(solution)/shard_map/all_gather | solution.py:156
  144.2 2.4 convolution_convert_fusion.2
  146.6 64.4 %all-reduce.4.cloned.1.call-done = bf16[256,224]{0,1:T(8,128)(2,1)} async-done(((bf16[256,224]{0,1:T(8,128)(2,1)}), bf16[256,224]{0,1:T(8,128)(2,1)}) %all-reduce.4.cloned.1.call-update) | async-done | bytes 114704 | tf_op jit(solution)/shard_map/psum | solution.py:158
  211.0 0.9 add_convert_fusion
  212.1 4.1 %gather_fusion.7 = bf16[1280,224]{1,0:T(8,128)(2,1)S(1)} fusion(bf16[128,224]{1,0:T(8,128)(2,1)S(1)} %copy.194, s32[2048]{0:T(1024)S(1)} %pad_clamp_fusion), kind=kCustom, calls=%fused_computation.7 | custom fusion | bytes 1152000 | tf_op jit(solution)/shard_map/jit(_take)/gather | solution.py:169
  216.2 1.2 select_select_fusion
  217.4 9.3 %all-to-all-start.1 = ((bf16[32,40,1,224]{3,1,2,0:T(8,128)(2,1)}), bf16[32,40,1,224]{3,1,2,0:T(8,128)(2,1)S(1)}, u32[]{:S(2)}, u32[]{:S(2)}) async-start(bf16[32,40,1,224]{3,1,2,0:T(8,128)(2,1)} %select_select_fusion), calls=%async_computation.1 | async-start | bytes 1310720 | tf_op jit(solution)/shard_map/all_to_all | solution.py:172
  226.8 17.8 %all-to-all-done.1 = bf16[32,40,1,224]{3,1,2,0:T(8,128)(2,1)S(1)} async-done(((bf16[32,40,1,224]{3,1,2,0:T(8,128)(2,1)}), bf16[32,40,1,224]{3,1,2,0:T(8,128)(2,1)S(1)}, u32[]{:S(2)}, u32[]{:S(2)}) %all-to-all-start.1) | async-done | bytes 573472 | tf_op jit(solution)/shard_map/all_to_all | solution.py:172
  244.7 0.8 copy-done.1
  245.4 1.5 copy.196
  246.9 2.1 reshape.672
  249.0 1.4 fusion.12
  250.4 2.9 fusion.91
  253.3 6.1 %convolution_convert_fusion = bf16[40,7168]{1,0:T(8,128)(2,1)} fusion(bf16[256,7168]{1,0:T(8,128)(2,1)} %param.29, bf16[7168,256]{1,0:T(8,128)(2,1)} %param.28, f32[40,256]{1,0:T(8,128)S(1)} %fusion.91, f32[40,7168]{1,0:T(8,128)S(1)} %reshape.672, f32[7168]{0:T(1024)S(1)} %copy-done.8, f32[40]{0:T(128)S(1)} %add_rsqrt_fusion), kind=kOutput, calls=%fused_computation.11 | convolution fusion | flops 294809600 | bytes 9130144 | tf_op jit(solution)/shard_map/dot_general | solution.py:182
  259.4 3.7 %convert_element_type.126 = bf16[1,40,128,56]{3,2,1,0:T(8,128)(2,1)S(1)} reshape(bf16[40,7168]{1,0:T(8,128)(2,1)} %convolution_convert_fusion) | data formatting | bytes 1146880 | tf_op jit(solution)/shard_map/convert_element_type | solution.py:184
  263.1 1.9 copy.237
  265.0 3.7 %reshape.761 = bf16[128,2,1120]{2,1,0:T(2,128)(2,1)} reshape(bf16[128,1,40,56]{3,2,1,0:T(8,128)(2,1)} %bitcast.155) | data formatting | bytes 1146880
  268.8 11.8 %all-to-all-start.2 = ((bf16[128,2,1120]{2,1,0:T(2,128)(2,1)}), bf16[128,2,1120]{2,1,0:T(2,128)(2,1)}, u32[]{:S(2)}, u32[]{:S(2)}) async-start(bf16[128,2,1120]{2,1,0:T(2,128)(2,1)} %reshape.761), calls=%async_computation.2 | async-start | bytes 1179648 | tf_op jit(solution)/shard_map/all_to_all | solution.py:183
  282.1 33.0 %gather_fusion.4 = f32[5120]{0:T(1024)S(1)} fusion(f32[128,16]{0,1:T(8,128)S(1)} %select_reduce_fusion.2, s32[5120]{0:T(1024)S(1)} %reshape.708), kind=kCustom, calls=%fused_computation.4 | custom fusion | bytes 81920 | tf_op jit(solution)/shard_map/gather | solution.py:205
  315.5 0.7 broadcast_select_fusion.1
  317.1 3.4 reshape.762
  320.5 1.7 bitcast_convert_fusion
  322.1 2.1 copy.217
  324.3 1.1 broadcast_multiply_fusion
  325.4 3.0 copy.200
  328.4 28.2 %scatter_fusion = f32[128,56]{1,0:T(8,128)S(1)} fusion(f32[128,56]{1,0:T(8,128)S(1)} %copy.199, s32[5120]{0:T(1024)S(1)} %copy-done.9, f32[5120,56]{1,0:T(8,128)} %copy.200), kind=kCustom, calls=%fused_computation.8 | custom fusion | flops 286720 | bytes 3461120 | tf_op jit(solution)/shard_map/scatter-add | solution.py:209
  (125 shorter events, 13.8 us)
Async XLA Ops:
  6.5 65.4 %copy-start = (bf16[16,512,128]{2,1,0:T(8,128)(2,1)S(1)}, bf16[16,512,128]{2,1,0:T(8,128)(2,1)}, u32[]{:S(2)}) copy-start(bf16[16,512,128]{2,1,0:T(8,128)(2,1)} %param.21) | copy-start | bytes 6291460
  11.4 13.0 %copy-start.14 = (s32[1,4]{1,0:T(1,128)S(1)}, s32[1,4]{1,0:T(1,128)}, u32[]{:S(2)}) copy-start(s32[1,4]{1,0:T(1,128)} %param.18) | copy-start | bytes 52
  11.4 13.3 %copy-start.10 = (bf16[8,576]{1,0:T(8,128)(2,1)S(1)}, bf16[8,576]{1,0:T(8,128)(2,1)}, u32[]{:S(2)}) copy-start(bf16[8,576]{1,0:T(8,128)(2,1)} %param.16) | copy-start | bytes 27652
  11.4 13.4 %copy-start.6 = (bf16[8,9216]{1,0:T(8,128)(2,1)S(1)}, bf16[8,9216]{1,0:T(8,128)(2,1)}, u32[]{:S(2)}) copy-start(bf16[8,9216]{1,0:T(8,128)(2,1)} %param.15) | copy-start | bytes 442372
  11.4 13.8 %copy-start.5 = (bf16[512,576]{0,1:T(8,128)(2,1)S(1)}, bf16[512,576]{0,1:T(8,128)(2,1)}, u32[]{:S(2)}) copy-start(bf16[512,576]{0,1:T(8,128)(2,1)} %param.17) | copy-start | bytes 1769476
  11.4 44.1 %all-to-all-start = ((bf16[32,2,16,576]{3,2,1,0:T(8,128)(2,1)}), bf16[32,2,16,576]{3,2,1,0:T(8,128)(2,1)}, u32[]{:S(2)}, u32[]{:S(2)}) async-start(bf16[32,2,16,576]{3,2,1,0:T(8,128)(2,1)} %copy.175), calls=%async_computation | async-start | bytes 2621440 | tf_op jit(solution)/shard_map/all_to_all | solution.py:97
  23.7 120.5 %all-gather.2.cloned.1.call-start = ((), (), s32[]{:S(2)}) async-start(), calls=%async_computation.3 | async-start | bytes 1081344 | tf_op jit(solution)/shard_map/all_gather | solution.py:156
  67.4 4.1 %copy-start.2 = (bf16[4,384,576]{2,1,0:T(8,128)(2,1)S(1)}, bf16[4,384,576]{2,1,0:T(8,128)(2,1)}, u32[]{:S(2)}) copy-start(bf16[4,384,576]{2,1,0:T(8,128)(2,1)} %get-tuple-element.12) | copy-start | bytes 5308420
  67.4 4.1 %copy-start.4 = (f32[4,2,16,384]{3,2,1,0:T(8,128)S(1)}, f32[4,2,16,384]{3,2,1,0:T(8,128)}, u32[]{:S(2)}) copy-start(f32[4,2,16,384]{3,2,1,0:T(8,128)} %get-tuple-element.28) | copy-start | bytes 589828
  72.0 1.4 copy-start.13
  72.0 72.2 %copy-start.3 = (bf16[2048,224]{0,1:T(8,128)(2,1)S(1)}, bf16[2048,224]{0,1:T(8,128)(2,1)}, u32[]{:S(2)}) copy-start(bf16[2048,224]{0,1:T(8,128)(2,1)} %param.22) | copy-start | bytes 2752516
  72.4 138.6 %copy-start.7 = (bf16[256,224]{0,1:T(8,128)(2,1)S(1)}, bf16[256,224]{0,1:T(8,128)(2,1)}, u32[]{:S(2)}) copy-start(bf16[256,224]{0,1:T(8,128)(2,1)} %param.23) | copy-start | bytes 344068
  73.1 137.9 %all-reduce.4.cloned.1.call-start = ((), (), s32[]{:S(2)}) async-start(), calls=%async_computation.4 | async-start | bytes 229376 | tf_op jit(solution)/shard_map/psum | solution.py:158
  217.4 27.2 %all-to-all-start.1 = ((bf16[32,40,1,224]{3,1,2,0:T(8,128)(2,1)}), bf16[32,40,1,224]{3,1,2,0:T(8,128)(2,1)S(1)}, u32[]{:S(2)}, u32[]{:S(2)}) async-start(bf16[32,40,1,224]{3,1,2,0:T(8,128)(2,1)} %select_select_fusion), calls=%async_computation.1 | async-start | bytes 1310720 | tf_op jit(solution)/shard_map/all_to_all | solution.py:172
  226.8 88.5 %copy-start.11 = (pred[128]{0:T(512)(128)(4,1)}, pred[128]{0:T(512)(128)(4,1)S(1)}, u32[]{:S(2)}) copy-start(pred[128]{0:T(512)(128)(4,1)S(1)} %compare_and_fusion.2) | copy-start | bytes 388
  244.6 0.9 copy-start.1
  246.9 3.5 copy-start.8
  265.0 16.8 %copy-start.12 = (f32[256,4]{0,1:T(4,128)S(1)}, f32[256,4]{0,1:T(4,128)}, u32[]{:S(2)}) copy-start(f32[256,4]{0,1:T(4,128)} %param.26) | copy-start | bytes 12292
  268.8 48.3 %all-to-all-start.2 = ((bf16[128,2,1120]{2,1,0:T(2,128)(2,1)}), bf16[128,2,1120]{2,1,0:T(2,128)(2,1)}, u32[]{:S(2)}, u32[]{:S(2)}) async-start(bf16[128,2,1120]{2,1,0:T(2,128)(2,1)} %reshape.761), calls=%async_computation.2 | async-start | bytes 1179648 | tf_op jit(solution)/shard_map/all_to_all | solution.py:183
  325.4 3.0 copy-start.9
Sparse Core Ops, SparseCore 0:
  73.2 70.9 all-gather.1
  146.7 64.2 all-reduce.3
where the time goes:
time: 365 us; the launch traced here: 364 us
  waiting for transfers between devices  164 us (45%)
  local copies, waits for them, and re-layouts  82.7 us (23%)
  other arithmetic  40.5 us (11%)
  starting transfers between devices  33.9 us (9%)
  matrix products  29.1 us (8%)
  between operations  14 us (4%)
    all_gather x1, waiting for transfers between devices, per_device(): lax.all_gather(values, 'attn', axis=0, tiled=True)  67.3 us
    psum x1, waiting for transfers between devices, per_device(): lax.psum(partial_cols.astype(jnp.bfloat16), ('expert', 'rep'))  64.4 us
    gather x2, local copies, waits for them, and re-layouts, per_device(): share_table[back_rows, source_expert[:, None]]  33.1 us
    scatter-add x1, other arithmetic, per_device(): jax.ops.segment_sum(weighted, back_rows.reshape(-1), num_segments=rows_part)  28.2 us
    all_to_all x1, waiting for transfers between devices, per_device(): lax.all_to_all(outgoing_rows, 'attn', split_axis=0, concat_axis=2, tiled=...  17.8 us
    all_to_all x1, waiting for transfers between devices, per_device(): lax.all_to_all(outgoing, 'attn', split_axis=0, concat_axis=0, tiled=True)  14.2 us
    all_to_all x1, starting transfers between devices, per_device(): lax.all_to_all(outgoing, 'attn', split_axis=0, concat_axis=0, tiled=True)  12.3 us
    all_to_all x1, starting transfers between devices, per_device(): lax.all_to_all(result.reshape(1, item_count, n_attn * n_expert, -1).astyp...  11.8 us
  transfers between devices with their start and end apart: 5, of which 4 were waited for; matrix products, arithmetic and copies ran while one was open for 16% of the time, Pallas kernels for 0%

commit v1 on v0

--- a/solution.py
+++ b/solution.py
@@ -11,6 +11,13 @@
 CAP = 2
 floor_score = -1e30
 scale_out = 2.5
+
+
+def gather_over(x, name, along):
+    peers = lax.axis_size(name)
+    blocks = jnp.stack([x for _ in range(peers)])
+    blocks = lax.all_to_all(blocks, name, split_axis=0, concat_axis=0)
+    return jnp.concatenate(blocks, axis=along)
 
 
 def expert_tables(route_ids, part_index, part_count, capacity):
@@ -152,9 +159,7 @@
         "rthc,hcv->rthv", attended, w_uv, preferred_element_type=jnp.float32
     ).astype(jnp.bfloat16)
     values = values.reshape(2 * req_count, head_count * w_uv.shape[2])
-    partial_cols = jnp.dot(
-        lax.all_gather(values, "attn", axis=0, tiled=True), w_o, preferred_element_type=jnp.float32
-    )
+    partial_cols = jnp.dot(gather_over(values, "attn", 0), w_o, preferred_element_type=jnp.float32)
     attn_cols = lax.psum(partial_cols.astype(jnp.bfloat16), ("expert", "rep")).astype(jnp.float32)
     hidden_cols = (residual.astype(jnp.float32) + attn_cols).astype(jnp.bfloat16)
     rows_part = route_ids.shape[0] // n_rep

time: 365 us -> 324 us (0.89)
  waiting for transfers between devices: 164 us -> 116 us
  starting transfers between devices: 33.9 us -> 39.6 us
    all_gather x1 -> x0, waiting for transfers between devices: 67.3 us -> none  [per_device(): lax.all_gather(values, 'attn', axis=0, tiled=True)]
    all_to_all x0 -> x1, waiting for transfers between devices: none -> 21.4 us  [gather_over(): blocks = lax.all_to_all(blocks, name, split_axis=0, concat_axis=0)]
    all_to_all x0 -> x1, starting transfers between devices: none -> 6.29 us  [gather_over(): blocks = lax.all_to_all(blocks, name, split_axis=0, concat_axis=0)]
    unnamed x34 -> x32, local copies, waits for them, and re-layouts: 9.59 us -> 8.99 us
  transfers between devices with their start and end apart: 5 -> 5, of which waited for: 4 -> 4; matrix products, arithmetic and copies ran while one was open for 16% -> 18% of each run, Pallas kernels for 0% -> 0%
where the time goes in v1:
time: 324 us; the launch traced here: 323 us
  waiting for transfers between devices  116 us (36%)
  local copies, waits for them, and re-layouts  83.2 us (26%)
  other arithmetic  40.5 us (12%)
  starting transfers between devices  39.6 us (12%)
  matrix products  29.1 us (9%)
  between operations  14 us (4%)
    psum x1, waiting for transfers between devices, per_device(): lax.psum(partial_cols.astype(jnp.bfloat16), ('expert', 'rep'))  62.5 us
    gather x2, local copies, waits for them, and re-layouts, per_device(): share_table[back_rows, source_expert[:, None]]  33.1 us
    scatter-add x1, other arithmetic, per_device(): jax.ops.segment_sum(weighted, back_rows.reshape(-1), num_segments=rows_part)  28.2 us
    all_to_all x1, waiting for transfers between devices, gather_over(): blocks = lax.all_to_all(blocks, name, split_axis=0, concat_axis=0)  21.4 us
    all_to_all x1, waiting for transfers between devices, per_device(): lax.all_to_all(outgoing_rows, 'attn', split_axis=0, concat_axis=2, tiled=...  17.8 us
    all_to_all x1, waiting for transfers between devices, per_device(): lax.all_to_all(outgoing, 'attn', split_axis=0, concat_axis=0, tiled=True)  14.5 us
    all_to_all x1, starting transfers between devices, per_device(): lax.all_to_all(outgoing, 'attn', split_axis=0, concat_axis=0, tiled=True)  12.3 us
    all_to_all x1, starting transfers between devices, per_device(): lax.all_to_all(result.reshape(1, item_count, n_attn * n_expert, -1).astyp...  11.5 us
  transfers between devices with their start and end apart: 5, of which 4 were waited for; matrix products, arithmetic and copies ran while one was open for 18% of the time, Pallas kernels for 0%

profile of v1, /device:TPU:1, one launch (start us, length us, event | category | flops | bytes accessed | tf_op | source)
XLA Modules:
  0.0 322.8 jit_solution(4314252654612775551)
XLA Ops:
  6.5 0.9 reshape.651
  7.5 0.8 convert_reduce_fusion
  8.3 1.6 convolution_convert_fusion.1
  9.9 1.5 copy.175
  11.4 12.3 %all-to-all-start = ((bf16[32,2,16,576]{3,2,1,0:T(8,128)(2,1)}), bf16[32,2,16,576]{3,2,1,0:T(8,128)(2,1)}, u32[]{:S(2)}, u32[]{:S(2)}) async-start(bf16[32,2,16,576]{3,2,1,0:T(8,128)(2,1)} %copy.175), calls=%async_computation | async-start | bytes 2621440 | tf_op jit(solution)/shard_map/all_to_all | solution.py:104
  25.0 1.1 copy.169
  26.0 2.4 gather_fusion
  28.4 1.2 concatenate.9
  30.1 8.1 %while.1 = (s32[]{:T(128)}, bf16[896,576]{1,0:T(8,128)(2,1)S(1)}, s32[4,2]{0,1:T(2,128)S(1)}, bf16[4,384,576]{2,1,0:T(8,128)(2,1)}, s32[]{:T(128)}) while((s32[]{:T(128)}, bf16[896,576]{1,0:T(8,128)(2,1)S(1)}, s32[4,2]{0,1:T(2,128)S(1)}, bf16[4,384,576]{2,1,0:T(8,128)(2,1)}, s32[]{:T(128)}) %tuple.22), condition=%wide.while_cond, body=%wide.while_body.sunk | while | flops 2 | bytes 935001 | solution.py:70
  30.6 1.5 bitcast_dynamic-update-slice_fusion.2
  32.7 1.5 bitcast_dynamic-update-slice_fusion.2
  34.7 1.4 bitcast_dynamic-update-slice_fusion.2
  36.7 1.5 bitcast_dynamic-update-slice_fusion.2
  38.1 3.0 fusion.94
  41.1 14.5 %all-to-all-done = bf16[32,2,16,576]{3,2,1,0:T(8,128)(2,1)} async-done(((bf16[32,2,16,576]{3,2,1,0:T(8,128)(2,1)}), bf16[32,2,16,576]{3,2,1,0:T(8,128)(2,1)}, u32[]{:S(2)}, u32[]{:S(2)}) %all-to-all-start) | async-done | bytes 1179680 | tf_op jit(solution)/shard_map/all_to_all | solution.py:104
  55.6 6.0 %fusion.2 = f32[64,2,16,16]{2,3,1,0:T(8,128)S(1)} fusion(bf16[64,16,576,1]{2,1,3,0:T(8,128)(2,1)} %bitcast.13, bf16[64,2,16,576]{3,2,1,0:T(8,128)(2,1)} %gather_fusion, pred[64]{0:T(512)(128)(4,1)S(1)} %compare_and_fusion.3), kind=kOutput, calls=%fused_computation.14 | convolution fusion | flops 38928384 | bytes 3670080 | tf_op jit(solution)/shard_map/nthc,nbc->nthb/dot_general | solution.py:115
  63.1 1.1 fusion.52
  64.7 0.9 copy.180
  65.5 1.9 fusion.43
  67.5 3.8 %fusion = f32[4,2,16,512]{3,0,2,1:T(4,128)S(1)} fusion(f32[64,2,16,512]{3,2,1,0:T(8,128)S(1)} %fusion.43, pred[4,64]{1,0:T(4,128)(4,1)S(1)} %fusion.82), kind=kOutput, calls=%fused_computation.12 | convolution fusion | flops 50331648 | bytes 4456704 | tf_op jit(solution)/shard_map/rn,nthc->rthc/dot_general | solution.py:154
  72.4 1.1 stack.3
  73.6 6.3 %all-to-all-start.1 = ((bf16[32,8,2048]{2,1,0:T(8,128)(2,1)}), bf16[32,8,2048]{2,1,0:T(8,128)(2,1)S(1)}, u32[]{:S(2)}, u32[]{:S(2)}) async-start(bf16[32,8,2048]{2,1,0:T(8,128)(2,1)} %stack.3), calls=%async_computation.1 | async-start | bytes 2097152 | tf_op jit(solution)/shard_map/all_to_all | solution.py:19
  80.5 0.8 select_reduce_fusion
  82.1 0.8 fusion.48
  83.7 21.4 %all-to-all-done.1 = bf16[32,8,2048]{2,1,0:T(8,128)(2,1)S(1)} async-done(((bf16[32,8,2048]{2,1,0:T(8,128)(2,1)}), bf16[32,8,2048]{2,1,0:T(8,128)(2,1)S(1)}, u32[]{:S(2)}, u32[]{:S(2)}) %all-to-all-start.1) | async-done | bytes 1048608 | tf_op jit(solution)/shard_map/all_to_all | solution.py:19
  105.1 2.3 convolution_convert_fusion.2
  107.5 62.5 %all-reduce.4.cloned.1.call-done = bf16[256,224]{0,1:T(8,128)(2,1)} async-done(((bf16[256,224]{0,1:T(8,128)(2,1)}), bf16[256,224]{0,1:T(8,128)(2,1)}) %all-reduce.4.cloned.1.call-update) | async-done | bytes 114704 | tf_op jit(solution)/shard_map/psum | solution.py:163
  170.0 0.9 add_convert_fusion
  171.0 4.1 %gather_fusion.7 = bf16[1280,224]{1,0:T(8,128)(2,1)S(1)} fusion(bf16[128,224]{1,0:T(8,128)(2,1)S(1)} %copy.194, s32[2048]{0:T(1024)S(1)} %pad_clamp_fusion), kind=kCustom, calls=%fused_computation.7 | custom fusion | bytes 1152000 | tf_op jit(solution)/shard_map/jit(_take)/gather | solution.py:174
  175.1 1.2 select_select_fusion
  176.3 9.3 %all-to-all-start.2 = ((bf16[32,40,1,224]{3,1,2,0:T(8,128)(2,1)}), bf16[32,40,1,224]{3,1,2,0:T(8,128)(2,1)S(1)}, u32[]{:S(2)}, u32[]{:S(2)}) async-start(bf16[32,40,1,224]{3,1,2,0:T(8,128)(2,1)} %select_select_fusion), calls=%async_computation.2 | async-start | bytes 1310720 | tf_op jit(solution)/shard_map/all_to_all | solution.py:177
  185.7 17.8 %all-to-all-done.2 = bf16[32,40,1,224]{3,1,2,0:T(8,128)(2,1)S(1)} async-done(((bf16[32,40,1,224]{3,1,2,0:T(8,128)(2,1)}), bf16[32,40,1,224]{3,1,2,0:T(8,128)(2,1)S(1)}, u32[]{:S(2)}, u32[]{:S(2)}) %all-to-all-start.2) | async-done | bytes 573472 | tf_op jit(solution)/shard_map/all_to_all | solution.py:177
  204.4 1.5 copy.196
  205.8 2.1 reshape.674
  207.9 1.4 fusion.12
  209.3 2.9 fusion.92
  212.2 6.1 %convolution_convert_fusion = bf16[40,7168]{1,0:T(8,128)(2,1)} fusion(bf16[256,7168]{1,0:T(8,128)(2,1)} %param.29, bf16[7168,256]{1,0:T(8,128)(2,1)} %param.28, f32[40,256]{1,0:T(8,128)S(1)} %fusion.92, f32[40,7168]{1,0:T(8,128)S(1)} %reshape.674, f32[7168]{0:T(1024)S(1)} %copy-done.7, f32[40]{0:T(128)S(1)} %add_rsqrt_fusion), kind=kOutput, calls=%fused_computation.11 | convolution fusion | flops 294809600 | bytes 9130144 | tf_op jit(solution)/shard_map/dot_general | solution.py:187
  218.3 3.7 %convert_element_type.126 = bf16[1,40,128,56]{3,2,1,0:T(8,128)(2,1)S(1)} reshape(bf16[40,7168]{1,0:T(8,128)(2,1)} %convolution_convert_fusion) | data formatting | bytes 1146880 | tf_op jit(solution)/shard_map/convert_element_type | solution.py:189
  222.0 1.9 copy.237
  223.9 3.7 %reshape.763 = bf16[128,2,1120]{2,1,0:T(2,128)(2,1)} reshape(bf16[128,1,40,56]{3,2,1,0:T(8,128)(2,1)} %bitcast.157) | data formatting | bytes 1146880
  227.7 11.5 %all-to-all-start.3 = ((bf16[128,2,1120]{2,1,0:T(2,128)(2,1)}), bf16[128,2,1120]{2,1,0:T(2,128)(2,1)}, u32[]{:S(2)}, u32[]{:S(2)}) async-start(bf16[128,2,1120]{2,1,0:T(2,128)(2,1)} %reshape.763), calls=%async_computation.3 | async-start | bytes 1179648 | tf_op jit(solution)/shard_map/all_to_all | solution.py:188
  240.8 33.0 %gather_fusion.4 = f32[5120]{0:T(1024)S(1)} fusion(f32[128,16]{0,1:T(8,128)S(1)} %select_reduce_fusion.2, s32[5120]{0:T(1024)S(1)} %reshape.710), kind=kCustom, calls=%fused_computation.4 | custom fusion | bytes 81920 | tf_op jit(solution)/shard_map/gather | solution.py:210
  275.8 3.4 %reshape.764 = bf16[128,1,40,56]{3,2,1,0:T(8,128)(2,1)S(1)} reshape(bf16[128,2,1120]{2,1,0:T(2,128)(2,1)} %all-to-all-done.3) | data formatting | bytes 1146880
  279.1 1.7 bitcast_convert_fusion
  280.8 2.1 copy.217
  282.9 1.1 broadcast_multiply_fusion
  284.0 3.0 copy.200
  287.0 28.2 %scatter_fusion = f32[128,56]{1,0:T(8,128)S(1)} fusion(f32[128,56]{1,0:T(8,128)S(1)} %copy.199, s32[5120]{0:T(1024)S(1)} %copy-done.8, f32[5120,56]{1,0:T(8,128)} %copy.200), kind=kCustom, calls=%fused_computation.8 | custom fusion | flops 286720 | bytes 3461120 | tf_op jit(solution)/shard_map/scatter-add | solution.py:214
  (123 shorter events, 14.4 us)
Async XLA Ops:
  6.5 65.4 %copy-start = (bf16[16,512,128]{2,1,0:T(8,128)(2,1)S(1)}, bf16[16,512,128]{2,1,0:T(8,128)(2,1)}, u32[]{:S(2)}) copy-start(bf16[16,512,128]{2,1,0:T(8,128)(2,1)} %param.21) | copy-start | bytes 6291460
  11.4 12.8 %copy-start.13 = (s32[1,4]{1,0:T(1,128)S(1)}, s32[1,4]{1,0:T(1,128)}, u32[]{:S(2)}) copy-start(s32[1,4]{1,0:T(1,128)} %param.18) | copy-start | bytes 52
  11.4 13.1 %copy-start.9 = (bf16[8,576]{1,0:T(8,128)(2,1)S(1)}, bf16[8,576]{1,0:T(8,128)(2,1)}, u32[]{:S(2)}) copy-start(bf16[8,576]{1,0:T(8,128)(2,1)} %param.16) | copy-start | bytes 27652
  11.4 13.1 %copy-start.5 = (bf16[8,9216]{1,0:T(8,128)(2,1)S(1)}, bf16[8,9216]{1,0:T(8,128)(2,1)}, u32[]{:S(2)}) copy-start(bf16[8,9216]{1,0:T(8,128)(2,1)} %param.15) | copy-start | bytes 442372
  11.4 13.5 %copy-start.4 = (bf16[512,576]{0,1:T(8,128)(2,1)S(1)}, bf16[512,576]{0,1:T(8,128)(2,1)}, u32[]{:S(2)}) copy-start(bf16[512,576]{0,1:T(8,128)(2,1)} %param.17) | copy-start | bytes 1769476
  11.4 44.1 %all-to-all-start = ((bf16[32,2,16,576]{3,2,1,0:T(8,128)(2,1)}), bf16[32,2,16,576]{3,2,1,0:T(8,128)(2,1)}, u32[]{:S(2)}, u32[]{:S(2)}) async-start(bf16[32,2,16,576]{3,2,1,0:T(8,128)(2,1)} %copy.175), calls=%async_computation | async-start | bytes 2621440 | tf_op jit(solution)/shard_map/all_to_all | solution.py:104
  67.4 4.1 %copy-start.2 = (bf16[4,384,576]{2,1,0:T(8,128)(2,1)S(1)}, bf16[4,384,576]{2,1,0:T(8,128)(2,1)}, u32[]{:S(2)}) copy-start(bf16[4,384,576]{2,1,0:T(8,128)(2,1)} %get-tuple-element.12) | copy-start | bytes 5308420
  67.4 4.1 %copy-start.3 = (f32[4,2,16,384]{3,2,1,0:T(8,128)S(1)}, f32[4,2,16,384]{3,2,1,0:T(8,128)}, u32[]{:S(2)}) copy-start(f32[4,2,16,384]{3,2,1,0:T(8,128)} %get-tuple-element.28) | copy-start | bytes 589828
  72.4 7.7 %copy-start.12 = (s32[256,4]{0,1:T(4,128)S(1)}, s32[256,4]{0,1:T(4,128)}, u32[]{:S(2)}) copy-start(s32[256,4]{0,1:T(4,128)} %param.25) | copy-start | bytes 12292
  73.6 31.5 %all-to-all-start.1 = ((bf16[32,8,2048]{2,1,0:T(8,128)(2,1)}), bf16[32,8,2048]{2,1,0:T(8,128)(2,1)S(1)}, u32[]{:S(2)}, u32[]{:S(2)}) async-start(bf16[32,8,2048]{2,1,0:T(8,128)(2,1)} %stack.3), calls=%async_computation.1 | async-start | bytes 2097152 | tf_op jit(solution)/shard_map/all_to_all | solution.py:19
  79.9 90.1 %copy-start.6 = (bf16[256,224]{0,1:T(8,128)(2,1)S(1)}, bf16[256,224]{0,1:T(8,128)(2,1)}, u32[]{:S(2)}) copy-start(bf16[256,224]{0,1:T(8,128)(2,1)} %param.23) | copy-start | bytes 344068
  79.9 90.1 %all-reduce.4.cloned.1.call-start = ((), (), s32[]{:S(2)}) async-start(), calls=%async_computation.4 | async-start | bytes 229376 | tf_op jit(solution)/shard_map/psum | solution.py:163
  176.3 27.2 %all-to-all-start.2 = ((bf16[32,40,1,224]{3,1,2,0:T(8,128)(2,1)}), bf16[32,40,1,224]{3,1,2,0:T(8,128)(2,1)S(1)}, u32[]{:S(2)}, u32[]{:S(2)}) async-start(bf16[32,40,1,224]{3,1,2,0:T(8,128)(2,1)} %select_select_fusion), calls=%async_computation.2 | async-start | bytes 1310720 | tf_op jit(solution)/shard_map/all_to_all | solution.py:177
  185.7 88.2 %copy-start.10 = (pred[128]{0:T(512)(128)(4,1)}, pred[128]{0:T(512)(128)(4,1)S(1)}, u32[]{:S(2)}) copy-start(pred[128]{0:T(512)(128)(4,1)S(1)} %compare_and_fusion.2) | copy-start | bytes 388
  203.5 0.9 copy-start.1
  205.8 3.5 %copy-start.7 = (f32[7168]{0:T(1024)S(1)}, f32[7168]{0:T(1024)}, u32[]{:S(2)}) copy-start(f32[7168]{0:T(1024)} %param.24) | copy-start | bytes 86020
  223.9 16.6 %copy-start.11 = (f32[256,4]{0,1:T(4,128)S(1)}, f32[256,4]{0,1:T(4,128)}, u32[]{:S(2)}) copy-start(f32[256,4]{0,1:T(4,128)} %param.26) | copy-start | bytes 12292
  227.7 48.1 %all-to-all-start.3 = ((bf16[128,2,1120]{2,1,0:T(2,128)(2,1)}), bf16[128,2,1120]{2,1,0:T(2,128)(2,1)}, u32[]{:S(2)}, u32[]{:S(2)}) async-start(bf16[128,2,1120]{2,1,0:T(2,128)(2,1)} %reshape.763), calls=%async_computation.3 | async-start | bytes 1179648 | tf_op jit(solution)/shard_map/all_to_all | solution.py:188
  284.0 3.0 copy-start.8
Sparse Core Ops, SparseCore 0:
  107.6 62.3 all-reduce.3
